TPU v7x, 32 devices: a whole 2x2x4 slice. The times are simulated.
32 devices in a mesh: grp: 2 (over y), chan: 4 (over z), tile: 2 (over x), sub: 2 (over core).
Axes of the slice: x: 2, y: 2, z: 4, core: 2. Of those that a mesh axis runs over, the one named last changes fastest.
Arguments:
- dirty: bfloat16 [128, 32, 8, 128], P(('grp', 'chan'), None, ('tile', 'sub')), parts along dimension 0, may hold values from -6 to 6
- cotangent: bfloat16 [128, 32, 8, 128], P(('grp', 'chan'), None, ('tile', 'sub')), parts along dimension 0, may hold values from -6 to 6
- spatial_kernel: float32 [32, 25], replicated, may hold values from -1.25 to 1.25
- feature_mix: bfloat16 [32, 32], replicated, may hold values from -1 to 1
- spectral_kernel: bfloat16 [7, 32, 32], replicated, may hold values from -0.375 to 0.375
- freq_table: int32 [64], replicated, may hold values from 0 to 63, as said below
Outputs:
- restored: bfloat16 [128, 32, 8, 128], P(('grp', 'chan'), None, ('tile', 'sub')), parts along dimension 0
- dirty_grad: bfloat16 [128, 32, 8, 128], P(('grp', 'chan'), None, ('tile', 'sub')), parts along dimension 0
- spatial_grad: float32 [64, 25], P('grp'), parts along dimension 0
- mix_grad: float32 [64, 32], P('grp'), parts along dimension 0
- spectral_grad: float32 [14, 32, 32], P('grp'), parts along dimension 0
There are 2 independent parts, one for each index of `grp`. A program takes and returns all parts, laid end to end along the dimension named above; an argument that names none is the same for every part. Nothing has to cross between parts.
Inputs may be any that keep to these rules, and one draw needn't show every extreme that they name: freq_table is a permutation of 0..63; the stored channels d * 16 to (d+1) * 16 - 1 hold exactly the frequencies m * 4 + d for m in 0..15, in any order.
All inputs are finite; a program needn't handle non-finite values.
Results may differ from a plain program's by a relative error of at most 0.0062.
Values may be sent and summed in bfloat16 or wider, within the bound.
No kernel may reach another device: no remote copies, remote signals or barrier semaphores. Data moves between devices by JAX's collectives and lax.ppermute only.
A program may use at most 64 MiB of HBM per device.

v0:
```python
import math
import jax
import jax.numpy as jnp
from jax import lax
from jax.sharding import PartitionSpec as P


def padded(block, sides, width):
    for axis, dim in sides:
        count = lax.axis_size(axis)
        forward = [(i, i + 1) for i in range(count - 1)]
        backward = [(target, source) for source, target in forward]
        low = lax.ppermute(
            lax.slice_in_dim(block, block.shape[dim] - width, None, axis=dim), axis, forward
        )
        high = lax.ppermute(lax.slice_in_dim(block, 0, width, axis=dim), axis, backward)
        block = jnp.concatenate([low, block, high], axis=dim)
    return block


def passed_along(block, axis, distance):
    devices = range(lax.axis_size(axis))
    route = [((i - distance) % len(devices), i) for i in devices]
    return lax.ppermute(block, axis, route)


def silu_slope(value):
    sig = jax.nn.sigmoid(value)
    return sig * (1.0 + value * (1.0 - sig))


def move_down(array):
    return jnp.pad(array, ((1, 0), (0, 0), (0, 0)))[:-1]


def move_up(array):
    return jnp.pad(array, ((0, 1), (0, 0), (0, 0)))[1:]


def local(dirty, cotangent, spatial_kernel, feature_mix, spectral_kernel, freq_table):
    chans, feats, rows, cols = dirty.shape
    taps = spectral_kernel.shape[0]
    half = (taps - 1) // 2
    n_chan = lax.axis_size("chan")
    n_rows = lax.axis_size("tile") * lax.axis_size("sub")
    scale = 1.0 / math.sqrt(chans * n_chan * rows * n_rows * cols)
    pixels = rows * cols
    extended = padded(dirty, ((("tile", "sub"), 2),), 2)
    xpad = jnp.pad(extended, ((0, 0), (0, 0), (0, 0), (2, 2)))
    xpad32 = xpad.astype(jnp.float32)
    total = jnp.zeros(dirty.shape, jnp.float32)
    for i in range(5):
        for j in range(5):
            total = (
                total
                + spatial_kernel[:, i * 5 + j][None, :, None, None]
                * xpad32[:, :, i : i + rows, j : j + cols]
            )
    smooth = total.astype(jnp.bfloat16)
    mixed = jnp.einsum("gf,cfhw->cghw", feature_mix, smooth, preferred_element_type=jnp.float32)
    hidden = jax.nn.silu(mixed).astype(jnp.bfloat16)
    hidden_flat = hidden.reshape(chans, feats, pixels)
    grad_flat = cotangent.reshape(chans, feats, pixels)
    device = lax.axis_index("chan")
    start = device * chans
    own = lax.dynamic_slice_in_dim(freq_table, start, chans) // n_chan
    order = jnp.zeros((chans,), jnp.int32).at[own].set(jnp.arange(chans, dtype=jnp.int32))
    h_sorted = hidden_flat[order]
    g_sorted = grad_flat[order]
    fwd_acc = jnp.einsum(
        "gf,mfp->mgp", spectral_kernel[half], h_sorted, preferred_element_type=jnp.float32
    )
    bwd_acc = jnp.einsum(
        "gf,mgp->mfp", spectral_kernel[half], g_sorted, preferred_element_type=jnp.float32
    )
    grad_taps = [None] * taps
    grad_taps[half] = jnp.einsum(
        "mgp,mfp->gf", g_sorted, h_sorted, preferred_element_type=jnp.float32
    )
    for dist in range(1, half + 1):
        for sign in (-1, 1):
            h_far, g_far = passed_along((h_sorted, g_sorted), "chan", -sign * dist)
            if sign < 0:
                wrapped = device < dist
                h_near = jnp.where(wrapped, move_down(h_far), h_far)
                g_near = jnp.where(wrapped, move_down(g_far), g_far)
            else:
                wrapped = device + dist >= n_chan
                h_near = jnp.where(wrapped, move_up(h_far), h_far)
                g_near = jnp.where(wrapped, move_up(g_far), g_far)
            offset = sign * dist
            fwd_acc = fwd_acc + jnp.einsum(
                "gf,mfp->mgp",
                spectral_kernel[half + offset],
                h_near,
                preferred_element_type=jnp.float32,
            )
            bwd_acc = bwd_acc + jnp.einsum(
                "gf,mgp->mfp",
                spectral_kernel[half - offset],
                g_near,
                preferred_element_type=jnp.float32,
            )
            grad_taps[half + offset] = jnp.einsum(
                "mgp,mfp->gf", g_sorted, h_near, preferred_element_type=jnp.float32
            )
    spec_grad = jnp.stack(grad_taps, 0)
    spec_flat = fwd_acc.astype(jnp.bfloat16)[own]
    back_flat = bwd_acc.astype(jnp.bfloat16)[own]
    spec = spec_flat.reshape(chans, feats, rows, cols)
    back = back_flat.reshape(chans, feats, rows, cols)
    restored = (dirty.astype(jnp.float32) + spec.astype(jnp.float32)).astype(jnp.bfloat16)
    dmixed = (back.astype(jnp.float32) * silu_slope(mixed)).astype(jnp.bfloat16)
    mix_term = jnp.einsum("cghw,cfhw->gf", dmixed, smooth, preferred_element_type=jnp.float32)
    dsmooth = jnp.einsum(
        "gf,cghw->cfhw", feature_mix, dmixed, preferred_element_type=jnp.float32
    ).astype(jnp.bfloat16)
    grad_ext = padded(dsmooth, ((("tile", "sub"), 2),), 2)
    dpad32 = jnp.pad(grad_ext, ((0, 0), (0, 0), (0, 0), (2, 2))).astype(jnp.float32)
    conv = jnp.zeros(dirty.shape, jnp.float32)
    terms = []
    for i in range(5):
        for j in range(5):
            conv = (
                conv
                + spatial_kernel[:, i * 5 + j][None, :, None, None]
                * dpad32[:, :, 4 - i : 4 - i + rows, 4 - j : 4 - j + cols]
            )
            terms.append(
                jnp.einsum(
                    "cfhw,cfhw->f",
                    dsmooth,
                    xpad[:, :, i : i + rows, j : j + cols],
                    preferred_element_type=jnp.float32,
                )
            )
    kernel_term = jnp.stack(terms, 1)
    dirty_grad = (cotangent.astype(jnp.float32) + conv).astype(jnp.bfloat16)
    kgrad, mgrad, sgrad = lax.psum((kernel_term, mix_term, spec_grad), ("chan", "tile", "sub"))
    return (restored, dirty_grad, kgrad * scale, mgrad * scale, sgrad * scale)


def solution(mesh):
    in_specs = (
        P(("grp", "chan"), None, ("tile", "sub"), None),
        P(("grp", "chan"), None, ("tile", "sub"), None),
        P(),
        P(),
        P(),
        P(),
    )
    out_specs = (
        P(("grp", "chan"), None, ("tile", "sub"), None),
        P(("grp", "chan"), None, ("tile", "sub"), None),
        P("grp", None),
        P("grp", None),
        P("grp", None, None),
    )
    return jax.shard_map(local, mesh=mesh, in_specs=in_specs, out_specs=out_specs, check_vma=False)
```

profile of v0, /device:TPU:0, one launch (start us, length us, event | category | flops | bytes accessed | tf_op | source)
XLA Modules:
  0.0 144.2 jit_solution(15052567029493651229)
XLA Ops:
  0.7 0.8 compare_select_fusion.1
  1.4 0.6 scatter_custom_fusion
  2.1 1.1 reshape.48
  3.2 0.6 gather_fusion.2
  3.8 4.1 %collective-permute-start.7 = (bf16[16,32,256]{2,1,0:T(8,128)(2,1)S(1)}, bf16[16,32,256]{2,1,0:T(8,128)(2,1)S(1)}, u32[]{:S(2)}, u32[]{:S(2)}) collective-permute-start(bf16[16,32,256]{2,1,0:T(8,128)(2,1)S(1)} %gather_fusion.2), channel_id=1, source_target_pairs={{8,0},{12,4},{0,8},{4,12},{9,1},{13,5},{1,9},{5,13},{10,2},{14,6},... | collective-permute-start | bytes 786440 | tf_op jit(solution)/shard_map/ppermute | solution.py:24
  7.9 1.3 collective-permute-start.6
  9.2 0.7 collective-permute-start.5
  9.9 1.0 copy.27
  10.9 1.3 collective-permute-start.1
  12.2 3.0 %collective-permute-start = (bf16[16,32,2,128]{3,1,2,0:T(8,128)(2,1)S(1)}, bf16[16,32,2,128]{3,1,2,0:T(8,128)(2,1)S(1)}, u32[]{:S(2)}, u32[]{:S(2)}) collective-permute-start(bf16[16,32,2,128]{3,1,2,0:T(8,128)(2,1)S(1)} %copy.27), channel_id=1, source_target_pairs={{0,1},{1,2},{2,3},{4,5},{5,6},{6,7},{8,9},{9,10},{10,11},{12,13},{... | collective-permute-start | bytes 786440 | tf_op jit(solution)/shard_map/ppermute | solution.py:13
  15.3 1.2 slice_reduce_fusion.23
  16.5 2.5 %slice_reduce_fusion.24 = (f32[32]{0:T(128)S(1)}, f32[32]{0:T(128)S(1)}, f32[32]{0:T(128)S(1)}, f32[32]{0:T(128)S(1)}, f32[32]{0:T(128)S(1)}, /*index=5*/f32[32]...) fusion(f32[32,25]{1,0:T(8,128)} %param.8), kind=kLoop, calls=%fused_computation.293 | loop fusion | bytes 4864 | tf_op jit(solution)/shard_map/slice | solution.py:56
  19.0 1.0 fusion.159
  20.0 1.5 %collective-permute-done.7 = bf16[16,32,256]{2,1,0:T(8,128)(2,1)S(1)} collective-permute-done((bf16[16,32,256]{2,1,0:T(8,128)(2,1)S(1)}, bf16[16,32,256]{2,1,0:T(8,128)(2,1)S(1)}, u32[]{:S(2)}, u32[]{:S(2)}) %collective-permute-start.7) | collective-permute-done | bytes 262176 | tf_op jit(solution)/shard_map/ppermute | solution.py:24
  21.5 1.0 fusion.109
  22.5 0.3 fusion.112
  22.8 3.9 %collective-permute-done.5 = bf16[16,32,256]{2,1,0:T(8,128)(2,1)S(1)} collective-permute-done((bf16[16,32,256]{2,1,0:T(8,128)(2,1)S(1)}, bf16[16,32,256]{2,1,0:T(8,128)(2,1)S(1)}, u32[]{:S(2)}, u32[]{:S(2)}) %collective-permute-start.5) | collective-permute-done | bytes 262176 | tf_op jit(solution)/shard_map/ppermute | solution.py:24
  26.6 0.3 fusion.118
  26.9 0.3 fusion.115
  27.2 0.3 convolution_add_fusion.3
  27.4 0.4 fusion.13
  27.9 0.6 gather_fusion.3
  28.5 0.8 select_maximum_fusion.2
  29.4 3.0 %fusion.74 = bf16[16,32,2,128]{3,1,2,0:T(8,128)(2,1)S(1)} fusion(f32[16,32,6,132]{3,1,2,0:T(8,128)S(1)} %get-tuple-element.72, f32[32]{0:T(128)S(1)} %get-tuple-element.66, f32[32]{0:T(128)S(1)} %get-tuple-element.67, f32[32]{0:T(128)S(1)} %get-tuple-element.44, f32[32]{0:T(128)S(1)} %get-tuple-element.45, f32[32]{0:T(128)S(1)} %get-tuple-element.46, ...), kind=kLoop, calls=%fused_computation.150 | loop fusion | flops 6553600 | bytes 13372544 | tf_op jit(solution)/shard_map/convert_element_type | solution.py:59
  32.4 1.1 fusion.46
  33.6 0.6 gather_fusion
  34.2 7.2 %collective-permute-start.4 = (bf16[16,32,256]{2,1,0:T(8,128)(2,1)S(1)}, bf16[16,32,256]{2,1,0:T(8,128)(2,1)}, u32[]{:S(2)}, u32[]{:S(2)}) collective-permute-start(bf16[16,32,256]{2,1,0:T(8,128)(2,1)S(1)} %gather_fusion), channel_id=1, source_target_pairs={{8,0},{12,4},{0,8},{4,12},{9,1},{13,5},{1,9},{5,13},{10,2},{14,6},... | collective-permute-start | bytes 786440 | tf_op jit(solution)/shard_map/ppermute | solution.py:24
  41.3 0.4 collective-permute-start.3
  41.8 1.6 %collective-permute-start.2 = (bf16[16,32,256]{2,1,0:T(8,128)(2,1)S(1)}, bf16[16,32,256]{2,1,0:T(8,128)(2,1)}, u32[]{:S(2)}, u32[]{:S(2)}) collective-permute-start(bf16[16,32,256]{2,1,0:T(8,128)(2,1)S(1)} %gather_fusion), channel_id=1, source_target_pairs={{12,0},{0,4},{4,8},{8,12},{13,1},{1,5},{5,9},{9,13},{14,2},{2,6},{... | collective-permute-start | bytes 786440 | tf_op jit(solution)/shard_map/ppermute | solution.py:24
  43.3 0.2 fusion.161
  43.6 2.5 %fusion.44 = (f32[32]{0:T(128)}, f32[32]{0:T(128)}, f32[32]{0:T(128)}, f32[32]{0:T(128)}, f32[32]{0:T(128)}, /*index=5*/f32[32]{0:T(128)}, bf16[16,2,128,32]{2,3,1,0:T(8,128)(2,1)S(1)}) fusion(bf16[16,32,6,132]{3,1,2,0:T(8,128)(2,1)S(1)} %get-tuple-element.71, bf16[16,32,2,128]{3,1,2,0:T(8,128)(2,1)} %copy-done.7, ...), kind=kOutput, calls=%fused_computation.93 | convolution fusion | flops 11272000 | bytes 1837824 | tf_op jit(solution)/shard_map/gf,cghw->cfhw/dot_general | solution.py:115
  46.0 2.3 %fusion.45 = (f32[32]{0:T(128)}, f32[32]{0:T(128)}, f32[32]{0:T(128)}, f32[32]{0:T(128)}, f32[32]{0:T(128)}, /*index=5*/f32[32]{0:T(128)}, f32[32]{0:T(128)}, f3...) fusion(bf16[16,32,6,132]{3,1,2,0:T(8,128)(2,1)S(1)} %get-tuple-, ...), kind=kLoop, calls=%fused_computation.94 | loop fusion | flops 7208384 | bytes 4983040 | tf_op jit(solution)/shard_map/cfhw,cfhw->f/dot_general | solution.py:130
  48.4 1.3 collective-permute-start.9
  49.7 3.0 %collective-permute-start.8 = (bf16[16,32,2,128]{3,1,2,0:T(8,128)(2,1)S(1)}, bf16[16,32,2,128]{3,1,2,0:T(8,128)(2,1)S(1)}, u32[]{:S(2)}, u32[]{:S(2)}) collective-permute-start(bf16[16,32,2,128]{3,1,2,0:T(8,128)(2,1)S(1)} %bitcast.338), channel_id=1, source_target_pairs={{0,1},{1,2},{2,3},{4,5},{5,6},{6,7},{8,9},{9,10},{10,11},{12,13},{... | collective-permute-start | bytes 786440 | tf_op jit(solution)/shard_map/ppermute | solution.py:13
  52.7 0.1 bitcast_convert_fusion
  52.8 0.2 convolution_bitcast_fusion.8
  53.0 0.8 multiply_reduce_fusion
  53.8 2.8 %stack.127 = f32[32,25]{0,1:T(8,128)S(1)} concatenate(f32[32,1]{0,1:T(1,128)} %bitcast.361, f32[32,1]{0,1:T(1,128)} %bitcast.359, f32[32,1]{0,1:T(1,128)} %bitcast.362, f32[32,1]{0,1:T(1,128)} %bitcast.358, f32[32,1]{0,1:T(1,128)} %bitcast.357, f32[32,1]{0,1:T(1,128)} %bitcast.356, f32[32,1]{0,1:T(1,128)} %bitcast.355, f32[32,1]{0,1:T(1,128)} %bitcast.363, f32[32,1]{0,1:T(1,128)} %bitcast.354, ...), dimensions={1} | concatenate | bytes 6400 | tf_op jit(solution)/shard_map/stack | solution.py:137
  56.6 3.7 %collective-permute-done.3 = bf16[16,32,256]{2,1,0:T(8,128)(2,1)} collective-permute-done((bf16[16,32,256]{2,1,0:T(8,128)(2,1)S(1)}, bf16[16,32,256]{2,1,0:T(8,128)(2,1)}, u32[]{:S(2)}, u32[]{:S(2)}) %collective-permute-start.3) | collective-permute-done | bytes 262176 | tf_op jit(solution)/shard_map/ppermute | solution.py:24
  60.3 1.3 fusion.21
  61.6 0.0 collective-permute-done.4
  61.6 1.3 fusion.20
  62.9 0.0 collective-permute-done.2
  63.0 1.3 fusion.19
  64.2 0.2 fusion.18
  64.5 1.3 fusion.17
  65.8 1.3 fusion.16
  67.1 1.3 fusion.15
  68.4 59.4 %all-reduce.14 = (f32[32,25]{0,1:T(8,128)S(1)}, f32[32,32]{1,0:T(8,128)S(1)}, f32[7,32,32]{2,1,0:T(8,128)S(1)}) all-reduce(f32[32,25]{0,1:T(8,128)S(1)} %stack.127, f32[32,32]{1,0:T(8,128)S(1)} %convolution_bitcast_fusion.8, f32[7,32,32]{2,1,0:T(8,128)S(1)} %fusion.15), channel_id=1, replica_groups=mesh['grp'=2,'chan'=4,'tile'=2,'sub'=2] {'chan','tile','sub'}, use_global_device_ids=true, to_apply=%region_1.2 | all-reduce | flops 8992 | bytes 71936 | tf_op jit(solution)/shard_map/psum | solution.py:139
  127.8 0.7 broadcast_multiply_fusion
  128.5 1.3 fusion.130
  129.8 1.3 fusion.136
  131.1 1.3 fusion.139
  132.4 1.3 fusion.133
  133.7 1.3 convolution_add_fusion.1
  135.0 1.3 fusion.14
  136.3 0.6 broadcast_multiply_fusion.1
  137.0 0.6 gather_fusion.1
  137.5 0.3 reshape.49
  137.8 0.7 copy.44
  138.5 1.0 add_convert_fusion
  139.5 0.7 fusion.1
  140.3 3.0 %fusion.49 = bf16[16,32,2,128]{3,1,2,0:T(8,128)(2,1)S(1)} fusion(f32[16,32,6,132]{3,1,2,0:T(8,128)S(1)} %fusion.1, bf16[16,32,2,128]{3,2,1,0:T(2,128)(2,1)S(1)} %copy-done.2, f32[32]{0:T(128)S(1)} %get-tuple-element.66, f32[32]{0:T(128)S(1)} %get-tuple-element.67, f32[32]{0:T(128)S(1)} %get-tuple-element.44, f32[32]{0:T(128)S(1)} %get-tuple-element.45, ...), kind=kLoop, calls=%fused_computation.100 | loop fusion | flops 6815744 | bytes 13634688 | tf_op jit(solution)/shard_map/convert_element_type | solution.py:138
  143.3 0.9 copy.43
  (57 shorter events, 0.2 us)
Async XLA Ops:
  0.6 31.8 %copy-start = (bf16[32,32]{1,0:T(8,128)(2,1)S(1)}, bf16[32,32]{1,0:T(8,128)(2,1)}, u32[]{:S(2)}) copy-start(bf16[32,32]{1,0:T(8,128)(2,1)} %param.9) | copy-start | bytes 6148
  0.6 21.9 %copy-start.8 = (bf16[7,32,32]{2,1,0:T(8,128)(2,1)S(1)}, bf16[7,32,32]{2,1,0:T(8,128)(2,1)}, u32[]{:S(2)}) copy-start(bf16[7,32,32]{2,1,0:T(8,128)(2,1)} %param.10) | copy-start | bytes 43012
  3.8 17.8 %collective-permute-start.7 = (bf16[16,32,256]{2,1,0:T(8,128)(2,1)S(1)}, bf16[16,32,256]{2,1,0:T(8,128)(2,1)S(1)}, u32[]{:S(2)}, u32[]{:S(2)}) collective-permute-start(bf16[16,32,256]{2,1,0:T(8,128)(2,1)S(1)} %gather_fusion.2), channel_id=1, source_target_pairs={{8,0},{12,4},{0,8},{4,12},{9,1},{13,5},{1,9},{5,13},{10,2},{14,6},... | collective-permute-start | bytes 786440 | tf_op jit(solution)/shard_map/ppermute | solution.py:24
  7.9 19.0 %collective-permute-start.6 = (bf16[16,32,256]{2,1,0:T(8,128)(2,1)S(1)}, bf16[16,32,256]{2,1,0:T(8,128)(2,1)S(1)}, u32[]{:S(2)}, u32[]{:S(2)}) collective-permute-start(bf16[16,32,256]{2,1,0:T(8,128)(2,1)S(1)} %gather_fusion.2), channel_id=1, source_target_pairs={{4,0},{8,4},{12,8},{0,12},{5,1},{9,5},{13,9},{1,13},{6,2},{10,6},{... | collective-permute-start | bytes 786440 | tf_op jit(solution)/shard_map/ppermute | solution.py:24
  9.2 17.4 %collective-permute-start.5 = (bf16[16,32,256]{2,1,0:T(8,128)(2,1)S(1)}, bf16[16,32,256]{2,1,0:T(8,128)(2,1)S(1)}, u32[]{:S(2)}, u32[]{:S(2)}) collective-permute-start(bf16[16,32,256]{2,1,0:T(8,128)(2,1)S(1)} %gather_fusion.2), channel_id=1, source_target_pairs={{12,0},{0,4},{4,8},{8,12},{13,1},{1,5},{5,9},{9,13},{14,2},{2,6},{... | collective-permute-start | bytes 786440 | tf_op jit(solution)/shard_map/ppermute | solution.py:24
  10.9 17.6 %copy-start.3 = (bf16[16,32,2,128]{3,1,2,0:T(8,128)(2,1)}, bf16[16,32,2,128]{3,1,2,0:T(8,128)(2,1)S(1)}, u32[]{:S(2)}) copy-start(bf16[16,32,2,128]{3,1,2,0:T(8,128)(2,1)S(1)} %copy.27) | copy-start | bytes 786436
  10.9 17.6 %collective-permute-start.1 = (bf16[16,32,2,128]{3,1,2,0:T(8,128)(2,1)S(1)}, bf16[16,32,2,128]{3,1,2,0:T(8,128)(2,1)S(1)}, u32[]{:S(2)}, u32[]{:S(2)}) collective-permute-start(bf16[16,32,2,128]{3,1,2,0:T(8,128)(2,1)S(1)} %copy.27), channel_id=1, source_target_pairs={{1,0},{2,1},{3,2},{5,4},{6,5},{7,6},{9,8},{10,9},{11,10},{13,12},{... | collective-permute-start | bytes 786440 | tf_op jit(solution)/shard_map/ppermute | solution.py:16
  12.2 16.3 %collective-permute-start = (bf16[16,32,2,128]{3,1,2,0:T(8,128)(2,1)S(1)}, bf16[16,32,2,128]{3,1,2,0:T(8,128)(2,1)S(1)}, u32[]{:S(2)}, u32[]{:S(2)}) collective-permute-start(bf16[16,32,2,128]{3,1,2,0:T(8,128)(2,1)S(1)} %copy.27), channel_id=1, source_target_pairs={{0,1},{1,2},{2,3},{4,5},{5,6},{6,7},{8,9},{9,10},{10,11},{12,13},{... | collective-permute-start | bytes 786440 | tf_op jit(solution)/shard_map/ppermute | solution.py:13
  27.8 1.5 %copy-start.9 = (f32[32]{0:T(128)S(1)}, f32[32]{0:T(128)}, u32[]{:S(2)}) copy-start(f32[32]{0:T(128)} %get-tuple-element.55) | copy-start | bytes 388
  27.8 1.5 %copy-start.11 = (f32[32]{0:T(128)S(1)}, f32[32]{0:T(128)}, u32[]{:S(2)}) copy-start(f32[32]{0:T(128)} %get-tuple-element.56) | copy-start | bytes 388
  27.8 1.5 %copy-start.13 = (f32[32]{0:T(128)S(1)}, f32[32]{0:T(128)}, u32[]{:S(2)}) copy-start(f32[32]{0:T(128)} %get-tuple-element.57) | copy-start | bytes 388
  27.8 1.5 %copy-start.15 = (f32[32]{0:T(128)S(1)}, f32[32]{0:T(128)}, u32[]{:S(2)}) copy-start(f32[32]{0:T(128)} %get-tuple-element.58) | copy-start | bytes 388
  27.9 1.5 %copy-start.17 = (f32[32]{0:T(128)S(1)}, f32[32]{0:T(128)}, u32[]{:S(2)}) copy-start(f32[32]{0:T(128)} %get-tuple-element.59) | copy-start | bytes 388
  27.9 1.5 %copy-start.19 = (f32[32]{0:T(128)S(1)}, f32[32]{0:T(128)}, u32[]{:S(2)}) copy-start(f32[32]{0:T(128)} %get-tuple-element.60) | copy-start | bytes 388
  27.9 1.5 %copy-start.21 = (f32[32]{0:T(128)S(1)}, f32[32]{0:T(128)}, u32[]{:S(2)}) copy-start(f32[32]{0:T(128)} %get-tuple-element.61) | copy-start | bytes 388
  28.5 3.9 %copy-start.6 = (bf16[16,32,2,128]{3,1,2,0:T(8,128)(2,1)}, bf16[16,32,2,128]{3,1,2,0:T(8,128)(2,1)S(1)}, u32[]{:S(2)}) copy-start(bf16[16,32,2,128]{3,1,2,0:T(8,128)(2,1)S(1)} %collective-permute-done.1) | copy-start | bytes 786436
  28.5 0.8 copy-start.7
  32.4 11.1 %copy-start.4 = (bf16[16,32,2,128]{3,1,2,0:T(8,128)(2,1)S(1)}, bf16[16,32,2,128]{3,1,2,0:T(8,128)(2,1)}, u32[]{:S(2)}) copy-start(bf16[16,32,2,128]{3,1,2,0:T(8,128)(2,1)} %copy-done.3) | copy-start | bytes 786436
  34.2 27.5 %collective-permute-start.4 = (bf16[16,32,256]{2,1,0:T(8,128)(2,1)S(1)}, bf16[16,32,256]{2,1,0:T(8,128)(2,1)}, u32[]{:S(2)}, u32[]{:S(2)}) collective-permute-start(bf16[16,32,256]{2,1,0:T(8,128)(2,1)S(1)} %gather_fusion), channel_id=1, source_target_pairs={{8,0},{12,4},{0,8},{4,12},{9,1},{13,5},{1,9},{5,13},{10,2},{14,6},... | collective-permute-start | bytes 786440 | tf_op jit(solution)/shard_map/ppermute | solution.py:24
  41.3 19.0 %collective-permute-start.3 = (bf16[16,32,256]{2,1,0:T(8,128)(2,1)S(1)}, bf16[16,32,256]{2,1,0:T(8,128)(2,1)}, u32[]{:S(2)}, u32[]{:S(2)}) collective-permute-start(bf16[16,32,256]{2,1,0:T(8,128)(2,1)S(1)} %gather_fusion), channel_id=1, source_target_pairs={{4,0},{8,4},{12,8},{0,12},{5,1},{9,5},{13,9},{1,13},{6,2},{10,6},{... | collective-permute-start | bytes 786440 | tf_op jit(solution)/shard_map/ppermute | solution.py:24
  41.8 21.2 %collective-permute-start.2 = (bf16[16,32,256]{2,1,0:T(8,128)(2,1)S(1)}, bf16[16,32,256]{2,1,0:T(8,128)(2,1)}, u32[]{:S(2)}, u32[]{:S(2)}) collective-permute-start(bf16[16,32,256]{2,1,0:T(8,128)(2,1)S(1)} %gather_fusion), channel_id=1, source_target_pairs={{12,0},{0,4},{4,8},{8,12},{13,1},{1,5},{5,9},{9,13},{14,2},{2,6},{... | collective-permute-start | bytes 786440 | tf_op jit(solution)/shard_map/ppermute | solution.py:24
  46.0 6.8 %copy-start.5 = (bf16[16,32,2,128]{3,1,2,0:T(8,128)(2,1)S(1)}, bf16[16,32,2,128]{3,1,2,0:T(8,128)(2,1)}, u32[]{:S(2)}) copy-start(bf16[16,32,2,128]{3,1,2,0:T(8,128)(2,1)} %get-tuple-element.73) | copy-start | bytes 786436
  46.0 7.0 %copy-start.1 = (bf16[16,32,2,128]{3,2,1,0:T(2,128)(2,1)S(1)}, bf16[16,32,2,128]{3,2,1,0:T(2,128)(2,1)}, u32[]{:S(2)}) copy-start(bf16[16,32,2,128]{3,2,1,0:T(2,128)(2,1)} %param.6) | copy-start | bytes 786436
  48.4 91.1 %collective-permute-start.9 = (bf16[16,32,2,128]{3,1,2,0:T(8,128)(2,1)S(1)}, bf16[16,32,2,128]{3,1,2,0:T(8,128)(2,1)S(1)}, u32[]{:S(2)}, u32[]{:S(2)}) collective-permute-start(bf16[16,32,2,128]{3,1,2,0:T(8,128)(2,1)S(1)} %bitcast.337), channel_id=1, source_target_pairs={{1,0},{2,1},{3,2},{5,4},{6,5},{7,6},{9,8},{10,9},{11,10},{13,12},{... | collective-permute-start | bytes 786440 | tf_op jit(solution)/shard_map/ppermute | solution.py:16
  49.7 89.8 %collective-permute-start.8 = (bf16[16,32,2,128]{3,1,2,0:T(8,128)(2,1)S(1)}, bf16[16,32,2,128]{3,1,2,0:T(8,128)(2,1)S(1)}, u32[]{:S(2)}, u32[]{:S(2)}) collective-permute-start(bf16[16,32,2,128]{3,1,2,0:T(8,128)(2,1)S(1)} %bitcast.338), channel_id=1, source_target_pairs={{0,1},{1,2},{2,3},{4,5},{5,6},{6,7},{8,9},{9,10},{10,11},{12,13},{... | collective-permute-start | bytes 786440 | tf_op jit(solution)/shard_map/ppermute | solution.py:13
  136.9 3.3 %copy-start.2 = (bf16[16,32,2,128]{3,2,1,0:T(2,128)(2,1)S(1)}, bf16[16,32,2,128]{3,2,1,0:T(2,128)(2,1)}, u32[]{:S(2)}) copy-start(bf16[16,32,2,128]{3,2,1,0:T(2,128)(2,1)} %param.7) | copy-start | bytes 786436
  136.9 3.3 %copy-start.10 = (f32[32]{0:T(128)S(1)}, f32[32]{0:T(128)}, u32[]{:S(2)}) copy-start(f32[32]{0:T(128)} %get-tuple-element.55) | copy-start | bytes 388
  136.9 3.3 %copy-start.12 = (f32[32]{0:T(128)S(1)}, f32[32]{0:T(128)}, u32[]{:S(2)}) copy-start(f32[32]{0:T(128)} %get-tuple-element.56) | copy-start | bytes 388
  136.9 3.3 %copy-start.14 = (f32[32]{0:T(128)S(1)}, f32[32]{0:T(128)}, u32[]{:S(2)}) copy-start(f32[32]{0:T(128)} %get-tuple-element.57) | copy-start | bytes 388
  136.9 3.3 %copy-start.16 = (f32[32]{0:T(128)S(1)}, f32[32]{0:T(128)}, u32[]{:S(2)}) copy-start(f32[32]{0:T(128)} %get-tuple-element.58) | copy-start | bytes 388
  136.9 3.3 %copy-start.18 = (f32[32]{0:T(128)S(1)}, f32[32]{0:T(128)}, u32[]{:S(2)}) copy-start(f32[32]{0:T(128)} %get-tuple-element.59) | copy-start | bytes 388
  136.9 3.3 %copy-start.20 = (f32[32]{0:T(128)S(1)}, f32[32]{0:T(128)}, u32[]{:S(2)}) copy-start(f32[32]{0:T(128)} %get-tuple-element.60) | copy-start | bytes 388
  137.0 3.3 %copy-start.22 = (f32[32]{0:T(128)S(1)}, f32[32]{0:T(128)}, u32[]{:S(2)}) copy-start(f32[32]{0:T(128)} %get-tuple-element.61) | copy-start | bytes 388
where the time goes:
time: 145 us; the launch traced here: 144 us
  blocking collectives  59.4 us (41%)
  starting transfers between devices  24 us (17%)
  matrix products  23.1 us (16%)
  other arithmetic  13.7 us (9%)
  local copies, waits for them, and re-layouts  13.6 us (9%)
  waiting for transfers between devices  9.18 us (6%)
    psum x1, blocking collectives, local(): lax.psum((kernel_term, mix_term, spec_grad), ('chan', 'tile', 'sub'))  59.4 us
    ppermute x6, starting transfers between devices, passed_along(): return lax.ppermute(block, axis, route)  15.3 us
    ppermute x6, waiting for transfers between devices, passed_along(): return lax.ppermute(block, axis, route)  9.17 us
    dot_general x6, matrix products, local(): jnp.einsum('gf,mfp->mgp', spectral_kernel[half + offset], h_near, preferr...  7.81 us
    dot_general x6, matrix products, local(): jnp.einsum('mgp,mfp->gf', g_sorted, h_near, preferred_element_type=jnp.fl...  7.77 us
    ppermute x2, starting transfers between devices, padded(): lax.ppermute(lax.slice_in_dim(block, block.shape[dim] - width, None, axis...  6.09 us
    slice x2, local copies, waits for them, and re-layouts, local(): spatial_kernel[:, i * 5 + j][None, :, None, None]  3.76 us
    dot_general x2, other arithmetic, local(): jnp.einsum('cfhw,cfhw->f', dsmooth, xpad[:, :, i:i + rows, j:j + cols], p...  3.12 us
  transfers between devices with their start and end apart: 10, of which 3 were waited for; matrix products, arithmetic and copies ran while one was open for 26% of the time, Pallas kernels for 0%

commit v1 on v0

--- a/solution.py
+++ b/solution.py
@@ -136,7 +136,9 @@
             )
     kernel_term = jnp.stack(terms, 1)
     dirty_grad = (cotangent.astype(jnp.float32) + conv).astype(jnp.bfloat16)
-    kgrad, mgrad, sgrad = lax.psum((kernel_term, mix_term, spec_grad), ("chan", "tile", "sub"))
+    kgrad, mgrad, sgrad = lax.psum(
+        lax.psum((kernel_term, mix_term, spec_grad), ("tile", "sub")), "chan"
+    )
     return (restored, dirty_grad, kgrad * scale, mgrad * scale, sgrad * scale)
 
 

time: 145 us -> 122 us (0.84)
  blocking collectives: 59.4 us -> 36.1 us
    psum x1 -> x2, blocking collectives: 59.4 us -> 36.1 us  [the longest x1 24.5 us: local(): lax.psum(lax.psum((kernel_term, mix_term, spec_grad), ('tile', 'sub')), '...]
  transfers between devices with their start and end apart: 10 -> 10, of which waited for: 3 -> 3; matrix products, arithmetic and copies ran while one was open for 26% -> 31% of each run, Pallas kernels for 0% -> 0%
where the time goes in v1:
time: 122 us; the launch traced here: 121 us
  blocking collectives  36.1 us (30%)
  starting transfers between devices  24 us (20%)
  matrix products  23.1 us (19%)
  other arithmetic  13.7 us (11%)
  local copies, waits for them, and re-layouts  13.6 us (11%)
  waiting for transfers between devices  9.18 us (8%)
  between operations  1.26 us (1%)
    psum x1, blocking collectives, local(): lax.psum(lax.psum((kernel_term, mix_term, spec_grad), ('tile', 'sub')), '...  24.5 us
    ppermute x6, starting transfers between devices, passed_along(): return lax.ppermute(block, axis, route)  15.3 us
    psum x1, blocking collectives, local(): lax.psum((kernel_term, mix_term, spec_grad), ('tile', 'sub'))  11.6 us
    ppermute x6, waiting for transfers between devices, passed_along(): return lax.ppermute(block, axis, route)  9.17 us
    dot_general x6, matrix products, local(): jnp.einsum('gf,mfp->mgp', spectral_kernel[half + offset], h_near, preferr...  7.81 us
    dot_general x6, matrix products, local(): jnp.einsum('mgp,mfp->gf', g_sorted, h_near, preferred_element_type=jnp.fl...  7.77 us
    ppermute x2, starting transfers between devices, padded(): lax.ppermute(lax.slice_in_dim(block, block.shape[dim] - width, None, axis...  6.09 us
    slice x2, local copies, waits for them, and re-layouts, local(): spatial_kernel[:, i * 5 + j][None, :, None, None]  3.76 us
  transfers between devices with their start and end apart: 10, of which 3 were waited for; matrix products, arithmetic and copies ran while one was open for 31% of the time, Pallas kernels for 0%

profile of v1, /device:TPU:0, one launch (start us, length us, event | category | flops | bytes accessed | tf_op | source)
XLA Modules:
  0.0 120.9 jit_solution(2755329282119038684)
XLA Ops:
  0.7 0.8 compare_select_fusion.1
  1.4 0.6 scatter_custom_fusion
  2.1 1.1 reshape.48
  3.2 0.6 gather_fusion.2
  3.8 4.1 %collective-permute-start.7 = (bf16[16,32,256]{2,1,0:T(8,128)(2,1)S(1)}, bf16[16,32,256]{2,1,0:T(8,128)(2,1)S(1)}, u32[]{:S(2)}, u32[]{:S(2)}) collective-permute-start(bf16[16,32,256]{2,1,0:T(8,128)(2,1)S(1)} %gather_fusion.2), channel_id=1, source_target_pairs={{8,0},{12,4},{0,8},{4,12},{9,1},{13,5},{1,9},{5,13},{10,2},{14,6},... | collective-permute-start | bytes 786440 | tf_op jit(solution)/shard_map/ppermute | solution.py:24
  7.9 1.3 %collective-permute-start.6 = (bf16[16,32,256]{2,1,0:T(8,128)(2,1)S(1)}, bf16[16,32,256]{2,1,0:T(8,128)(2,1)S(1)}, u32[]{:S(2)}, u32[]{:S(2)}) collective-permute-start(bf16[16,32,256]{2,1,0:T(8,128)(2,1)S(1)} %gather_fusion.2), channel_id=1, source_target_pairs={{4,0},{8,4},{12,8},{0,12},{5,1},{9,5},{13,9},{1,13},{6,2},{10,6},{... | collective-permute-start | bytes 786440 | tf_op jit(solution)/shard_map/ppermute | solution.py:24
  9.2 0.7 collective-permute-start.5
  9.9 1.0 copy.27
  10.9 1.3 %collective-permute-start.1 = (bf16[16,32,2,128]{3,1,2,0:T(8,128)(2,1)S(1)}, bf16[16,32,2,128]{3,1,2,0:T(8,128)(2,1)S(1)}, u32[]{:S(2)}, u32[]{:S(2)}) collective-permute-start(bf16[16,32,2,128]{3,1,2,0:T(8,128)(2,1)S(1)} %copy.27), channel_id=1, source_target_pairs={{1,0},{2,1},{3,2},{5,4},{6,5},{7,6},{9,8},{10,9},{11,10},{13,12},{... | collective-permute-start | bytes 786440 | tf_op jit(solution)/shard_map/ppermute | solution.py:16
  12.2 3.0 %collective-permute-start = (bf16[16,32,2,128]{3,1,2,0:T(8,128)(2,1)S(1)}, bf16[16,32,2,128]{3,1,2,0:T(8,128)(2,1)S(1)}, u32[]{:S(2)}, u32[]{:S(2)}) collective-permute-start(bf16[16,32,2,128]{3,1,2,0:T(8,128)(2,1)S(1)} %copy.27), channel_id=1, source_target_pairs={{0,1},{1,2},{2,3},{4,5},{5,6},{6,7},{8,9},{9,10},{10,11},{12,13},{... | collective-permute-start | bytes 786440 | tf_op jit(solution)/shard_map/ppermute | solution.py:13
  15.3 1.2 %slice_reduce_fusion.23 = (f32[32]{0:T(128)S(1)}, f32[32]{0:T(128)S(1)}, f32[32]{0:T(128)S(1)}, f32[32]{0:T(128)S(1)}, f32[32]{0:T(128)S(1)}, /*index=5*/f32[32]{0:T(128)S(1)}) fusion(f32[32,25]{1,0:T(8,128)} %param.8), kind=kLoop, calls=%fused_computation.292 | loop fusion | bytes 1536 | tf_op jit(solution)/shard_map/slice | solution.py:56
  16.5 2.5 %slice_reduce_fusion.24 = (f32[32]{0:T(128)S(1)}, f32[32]{0:T(128)S(1)}, f32[32]{0:T(128)S(1)}, f32[32]{0:T(128)S(1)}, f32[32]{0:T(128)S(1)}, /*index=5*/f32[32]...) fusion(f32[32,25]{1,0:T(8,128)} %param.8), kind=kLoop, calls=%fused_computation.293 | loop fusion | bytes 4864 | tf_op jit(solution)/shard_map/slice | solution.py:56
  19.0 1.0 fusion.159
  20.0 1.5 %collective-permute-done.7 = bf16[16,32,256]{2,1,0:T(8,128)(2,1)S(1)} collective-permute-done((bf16[16,32,256]{2,1,0:T(8,128)(2,1)S(1)}, bf16[16,32,256]{2,1,0:T(8,128)(2,1)S(1)}, u32[]{:S(2)}, u32[]{:S(2)}) %collective-permute-start.7) | collective-permute-done | bytes 262176 | tf_op jit(solution)/shard_map/ppermute | solution.py:24
  21.5 1.0 fusion.109
  22.5 0.3 fusion.112
  22.8 3.9 %collective-permute-done.5 = bf16[16,32,256]{2,1,0:T(8,128)(2,1)S(1)} collective-permute-done((bf16[16,32,256]{2,1,0:T(8,128)(2,1)S(1)}, bf16[16,32,256]{2,1,0:T(8,128)(2,1)S(1)}, u32[]{:S(2)}, u32[]{:S(2)}) %collective-permute-start.5) | collective-permute-done | bytes 262176 | tf_op jit(solution)/shard_map/ppermute | solution.py:24
  26.6 0.3 fusion.118
  26.9 0.3 fusion.115
  27.2 0.3 convolution_add_fusion.3
  27.4 0.4 fusion.13
  27.9 0.6 gather_fusion.3
  28.5 0.8 select_maximum_fusion.2
  29.4 3.0 %fusion.74 = bf16[16,32,2,128]{3,1,2,0:T(8,128)(2,1)S(1)} fusion(f32[16,32,6,132]{3,1,2,0:T(8,128)S(1)} %get-tuple-element.75, f32[32]{0:T(128)S(1)} %get-tuple-element.66, f32[32]{0:T(128)S(1)} %get-tuple-element.67, f32[32]{0:T(128)S(1)} %get-tuple-element.44, f32[32]{0:T(128)S(1)} %get-tuple-element.45, f32[32]{0:T(128)S(1)} %get-tuple-element.46, ...), kind=kLoop, calls=%fused_computation.150 | loop fusion | flops 6553600 | bytes 13372544 | tf_op jit(solution)/shard_map/convert_element_type | solution.py:59
  32.4 1.1 fusion.46
  33.6 0.6 gather_fusion
  34.2 7.2 %collective-permute-start.4 = (bf16[16,32,256]{2,1,0:T(8,128)(2,1)S(1)}, bf16[16,32,256]{2,1,0:T(8,128)(2,1)}, u32[]{:S(2)}, u32[]{:S(2)}) collective-permute-start(bf16[16,32,256]{2,1,0:T(8,128)(2,1)S(1)} %gather_fusion), channel_id=1, source_target_pairs={{8,0},{12,4},{0,8},{4,12},{9,1},{13,5},{1,9},{5,13},{10,2},{14,6},... | collective-permute-start | bytes 786440 | tf_op jit(solution)/shard_map/ppermute | solution.py:24
  41.3 0.4 collective-permute-start.3
  41.8 1.6 %collective-permute-start.2 = (bf16[16,32,256]{2,1,0:T(8,128)(2,1)S(1)}, bf16[16,32,256]{2,1,0:T(8,128)(2,1)}, u32[]{:S(2)}, u32[]{:S(2)}) collective-permute-start(bf16[16,32,256]{2,1,0:T(8,128)(2,1)S(1)} %gather_fusion), channel_id=1, source_target_pairs={{12,0},{0,4},{4,8},{8,12},{13,1},{1,5},{5,9},{9,13},{14,2},{2,6},{... | collective-permute-start | bytes 786440 | tf_op jit(solution)/shard_map/ppermute | solution.py:24
  43.3 0.2 fusion.161
  43.6 2.5 %fusion.44 = (f32[32]{0:T(128)}, f32[32]{0:T(128)}, f32[32]{0:T(128)}, f32[32]{0:T(128)}, f32[32]{0:T(128)}, /*index=5*/f32[32]{0:T(128)}, bf16[16,2,128,32]{2,3,1,0:T(8,128)(2,1)S(1)}) fusion(bf16[16,32,6,132]{3,1,2,0:T(8,128)(2,1)S(1)} %get-tuple-element.74, bf16[16,32,2,128]{3,1,2,0:T(8,128)(2,1)} %copy-done.7, ...), kind=kOutput, calls=%fused_computation.93 | convolution fusion | flops 11272000 | bytes 1837824 | tf_op jit(solution)/shard_map/gf,cghw->cfhw/dot_general | solution.py:115
  46.0 2.3 %fusion.45 = (f32[32]{0:T(128)}, f32[32]{0:T(128)}, f32[32]{0:T(128)}, f32[32]{0:T(128)}, f32[32]{0:T(128)}, /*index=5*/f32[32]{0:T(128)}, f32[32]{0:T(128)}, f3...) fusion(bf16[16,32,6,132]{3,1,2,0:T(8,128)(2,1)S(1)} %get-tuple-, ...), kind=kLoop, calls=%fused_computation.94 | loop fusion | flops 7208384 | bytes 4983040 | tf_op jit(solution)/shard_map/cfhw,cfhw->f/dot_general | solution.py:130
  48.4 1.3 %collective-permute-start.9 = (bf16[16,32,2,128]{3,1,2,0:T(8,128)(2,1)S(1)}, bf16[16,32,2,128]{3,1,2,0:T(8,128)(2,1)S(1)}, u32[]{:S(2)}, u32[]{:S(2)}) collective-permute-start(bf16[16,32,2,128]{3,1,2,0:T(8,128)(2,1)S(1)} %bitcast.337), channel_id=1, source_target_pairs={{1,0},{2,1},{3,2},{5,4},{6,5},{7,6},{9,8},{10,9},{11,10},{13,12},{... | collective-permute-start | bytes 786440 | tf_op jit(solution)/shard_map/ppermute | solution.py:16
  49.7 3.0 %collective-permute-start.8 = (bf16[16,32,2,128]{3,1,2,0:T(8,128)(2,1)S(1)}, bf16[16,32,2,128]{3,1,2,0:T(8,128)(2,1)S(1)}, u32[]{:S(2)}, u32[]{:S(2)}) collective-permute-start(bf16[16,32,2,128]{3,1,2,0:T(8,128)(2,1)S(1)} %bitcast.338), channel_id=1, source_target_pairs={{0,1},{1,2},{2,3},{4,5},{5,6},{6,7},{8,9},{9,10},{10,11},{12,13},{... | collective-permute-start | bytes 786440 | tf_op jit(solution)/shard_map/ppermute | solution.py:13
  52.7 0.1 bitcast_convert_fusion
  52.8 0.2 convolution_bitcast_fusion.8
  53.0 0.8 multiply_reduce_fusion
  53.8 2.8 %stack.127 = f32[32,25]{0,1:T(8,128)S(1)} concatenate(f32[32,1]{0,1:T(1,128)} %bitcast.361, f32[32,1]{0,1:T(1,128)} %bitcast.359, f32[32,1]{0,1:T(1,128)} %bitcast.362, f32[32,1]{0,1:T(1,128)} %bitcast.358, f32[32,1]{0,1:T(1,128)} %bitcast.357, f32[32,1]{0,1:T(1,128)} %bitcast.356, f32[32,1]{0,1:T(1,128)} %bitcast.355, f32[32,1]{0,1:T(1,128)} %bitcast.363, f32[32,1]{0,1:T(1,128)} %bitcast.354, ...), dimensions={1} | concatenate | bytes 6400 | tf_op jit(solution)/shard_map/stack | solution.py:137
  56.6 3.7 %collective-permute-done.3 = bf16[16,32,256]{2,1,0:T(8,128)(2,1)} collective-permute-done((bf16[16,32,256]{2,1,0:T(8,128)(2,1)S(1)}, bf16[16,32,256]{2,1,0:T(8,128)(2,1)}, u32[]{:S(2)}, u32[]{:S(2)}) %collective-permute-start.3) | collective-permute-done | bytes 262176 | tf_op jit(solution)/shard_map/ppermute | solution.py:24
  60.3 1.3 %fusion.21 = f32[7,32,32]{2,1,0:T(8,128)S(1)} fusion(bf16[16,32,256]{2,1,0:T(8,128)(2,1)S(1)} %gather_fusion.2, bf16[16,32,256]{2,1,0:T(8,128)(2,1)} %collective-permute-done.3, pred[]{:T(512)S(6)} %lt.26), kind=kOutput, calls=%fused_computation.69 | convolution fusion | flops 8519679 | bytes 540673 | tf_op jit(solution)/shard_map/mgp,mfp->gf/dot_general | solution.py:104
  61.6 0.0 collective-permute-done.4
  61.6 1.3 %fusion.20 = f32[7,32,32]{2,1,0:T(8,128)S(1)} fusion(f32[7,32,32]{2,1,0:T(8,128)S(1)} %fusion.21, bf16[16,32,256]{2,1,0:T(8,128)(2,1)S(1)} %gather_fusion.2, bf16[16,32,256]{2,1,0:T(8,128)(2,1)} %collective-permute-done.4, pred[]{:T(512)S(6)} %lt.25), kind=kOutput, calls=%fused_computation.67 | convolution fusion | flops 8519680 | bytes 540673 | tf_op jit(solution)/shard_map/mgp,mfp->gf/dot_general | solution.py:104
  63.0 1.3 %fusion.19 = f32[7,32,32]{2,1,0:T(8,128)S(1)} fusion(f32[7,32,32]{2,1,0:T(8,128)S(1)} %fusion.20, bf16[16,32,256]{2,1,0:T(8,128)(2,1)S(1)} %gather_fusion.2, bf16[16,32,256]{2,1,0:T(8,128)(2,1)} %collective-permute-done.2, pred[]{:T(512)S(6)} %lt.24), kind=kOutput, calls=%fused_computation.65 | convolution fusion | flops 8519680 | bytes 540673 | tf_op jit(solution)/shard_map/mgp,mfp->gf/dot_general | solution.py:104
  64.2 0.2 fusion.18
  64.5 1.3 %fusion.17 = f32[7,32,32]{2,1,0:T(8,128)S(1)} fusion(f32[7,32,32]{2,1,0:T(8,128)S(1)} %fusion.18, bf16[16,32,256]{2,1,0:T(8,128)(2,1)S(1)} %gather_fusion.2, bf16[16,32,256]{2,1,0:T(8,128)(2,1)} %collective-permute-done.3, pred[]{:T(512)S(6)} %ge.9), kind=kOutput, calls=%fused_computation.61 | convolution fusion | flops 8519680 | bytes 540673 | tf_op jit(solution)/shard_map/mgp,mfp->gf/dot_general | solution.py:104
  65.8 1.3 %fusion.16 = f32[7,32,32]{2,1,0:T(8,128)S(1)} fusion(f32[7,32,32]{2,1,0:T(8,128)S(1)} %fusion.17, bf16[16,32,256]{2,1,0:T(8,128)(2,1)S(1)} %gather_fusion.2, bf16[16,32,256]{2,1,0:T(8,128)(2,1)} %collective-permute-done.4, pred[]{:T(512)S(6)} %ge.10), kind=kOutput, calls=%fused_computation.59 | convolution fusion | flops 8519680 | bytes 540673 | tf_op jit(solution)/shard_map/mgp,mfp->gf/dot_general | solution.py:104
  67.1 1.3 %fusion.15 = f32[7,32,32]{2,1,0:T(8,128)S(1)} fusion(f32[7,32,32]{2,1,0:T(8,128)S(1)} %fusion.16, bf16[16,32,256]{2,1,0:T(8,128)(2,1)S(1)} %gather_fusion.2, bf16[16,32,256]{2,1,0:T(8,128)(2,1)} %collective-permute-done.2, pred[]{:T(512)S(6)} %ge.11), kind=kOutput, calls=%fused_computation.57 | convolution fusion | flops 8519680 | bytes 540673 | tf_op jit(solution)/shard_map/mgp,mfp->gf/dot_general | solution.py:104
  68.4 11.6 %all-reduce.14 = (f32[32,25]{0,1:T(8,128)S(1)}, f32[32,32]{1,0:T(8,128)S(1)}, f32[7,32,32]{2,1,0:T(8,128)S(1)}) all-reduce(f32[32,25]{0,1:T(8,128)S(1)} %stack.127, f32[32,32]{1,0:T(8,128)S(1)} %convolution_bitcast_fusion.8, f32[7,32,32]{2,1,0:T(8,128)S(1)} %fusion.15), channel_id=1, replica_groups=mesh['grp'=2,'chan'=4,'tile'=2,'sub'=2] {'tile','sub'}, use_global_device_ids=true, to_apply=%region_1.2 | all-reduce | flops 8992 | bytes 71936 | tf_op jit(solution)/shard_map/psum | solution.py:140
  79.9 24.5 %all-reduce.15 = (f32[32,25]{0,1:T(8,128)S(1)}, f32[32,32]{1,0:T(8,128)S(1)}, f32[7,32,32]{2,1,0:T(8,128)S(1)}) all-reduce(f32[32,25]{0,1:T(8,128)S(1)} %get-tuple-element.68, f32[32,32]{1,0:T(8,128)S(1)} %get-tuple-element.69, f32[7,32,32]{2,1,0:T(8,128)S(1)} %get-tuple-element.70), channel_id=1, replica_groups=mesh['grp'=2,'chan'=4,'tile'=2,'sub'=2] {'chan'}, use_global_device_ids=true, to_apply=%region_2.3 | all-reduce | flops 8992 | bytes 71936 | tf_op jit(solution)/shard_map/psum | solution.py:139
  104.5 0.7 broadcast_multiply_fusion
  105.1 1.3 %fusion.130 = f32[16,256,32]{1,2,0:T(8,128)S(1)} fusion(bf16[16,32,256]{2,1,0:T(8,128)(2,1)} %collective-permute-done.2, pred[]{:T(512)S(6)} %ge.11, bf16[7,32,32]{2,1,0:T(8,128)(2,1)S(1)} %copy-done.8), kind=kOutput, calls=%fused_computation.265 | convolution fusion | flops 8519680 | bytes 794625 | tf_op jit(solution)/shard_map/gf,mfp->mgp/dot_general | solution.py:92
  106.4 1.3 %fusion.136 = f32[16,256,32]{1,2,0:T(8,128)S(1)} fusion(bf16[16,32,256]{2,1,0:T(8,128)(2,1)} %collective-permute-done.4, pred[]{:T(512)S(6)} %ge.10, bf16[7,32,32]{2,1,0:T(8,128)(2,1)S(1)} %copy-done.8), kind=kOutput, calls=%fused_computation.267 | convolution fusion | flops 8519680 | bytes 794625 | tf_op jit(solution)/shard_map/gf,mfp->mgp/dot_general | solution.py:92
  107.7 1.3 %fusion.139 = f32[16,256,32]{1,2,0:T(8,128)S(1)} fusion(bf16[16,32,256]{2,1,0:T(8,128)(2,1)} %collective-permute-done.4, pred[]{:T(512)S(6)} %lt.25, bf16[7,32,32]{2,1,0:T(8,128)(2,1)S(1)} %copy-done.8), kind=kOutput, calls=%fused_computation.268 | convolution fusion | flops 8519680 | bytes 794625 | tf_op jit(solution)/shard_map/gf,mfp->mgp/dot_general | solution.py:92
  109.0 1.3 %fusion.133 = f32[16,256,32]{1,2,0:T(8,128)S(1)} fusion(bf16[16,32,256]{2,1,0:T(8,128)(2,1)} %collective-permute-done.3, pred[]{:T(512)S(6)} %lt.26, bf16[7,32,32]{2,1,0:T(8,128)(2,1)S(1)} %copy-done.8), kind=kOutput, calls=%fused_computation.266 | convolution fusion | flops 8519680 | bytes 794625 | tf_op jit(solution)/shard_map/gf,mfp->mgp/dot_general | solution.py:92
  110.3 1.3 %convolution_add_fusion.1 = f32[16,256,32]{1,2,0:T(8,128)S(1)} fusion(f32[16,256,32]{1,2,0:T(8,128)S(1)} %fusion.161, bf16[16,32,256]{2,1,0:T(8,128)(2,1)} %collective-permute-done.2, pred[]{:T(512)S(6)} %lt.24, bf16[7,32,32]{2,1,0:T(8,128)(2,1)S(1)} %copy-done.8), kind=kOutput, calls=%fused_computation.39 | convolution fusion | flops 8650752 | bytes 1318913 | tf_op jit(solution)/shard_map/gf,mfp->mgp/dot_general | solution.py:92
  111.6 1.3 %fusion.14 = bf16[16,32,256]{2,1,0:T(8,128)(2,1)S(1)} fusion(f32[16,256,32]{1,2,0:T(8,128)S(1)} %fusion.130, f32[16,256,32]{1,2,0:T(8,128)S(1)} %fusion.133, f32[16,256,32]{1,2,0:T(8,128)S(1)} %fusion.136, f32[16,256,32]{1,2,0:T(8,128)S(1)} %fusion.139, f32[16,256,32]{1,2,0:T(8,128)S(1)} %convolution_add_fusion.1, ...), kind=kOutput, calls=%fused_computation.55 | convolution fusion | flops 9306112 | bytes 3153921 | tf_op jit(solution)/shard_map/gf,mfp->mgp/dot_general | solution.py:92
  113.0 0.6 broadcast_multiply_fusion.1
  113.6 0.6 gather_fusion.1
  114.2 0.3 reshape.49
  114.5 0.7 copy.44
  115.1 1.0 add_convert_fusion
  116.1 0.7 fusion.1
  116.9 3.0 %fusion.49 = bf16[16,32,2,128]{3,1,2,0:T(8,128)(2,1)S(1)} fusion(f32[16,32,6,132]{3,1,2,0:T(8,128)S(1)} %fusion.1, bf16[16,32,2,128]{3,2,1,0:T(2,128)(2,1)S(1)} %copy-done.2, f32[32]{0:T(128)S(1)} %get-tuple-element.66, f32[32]{0:T(128)S(1)} %get-tuple-element.67, f32[32]{0:T(128)S(1)} %get-tuple-element.44, f32[32]{0:T(128)S(1)} %get-tuple-element.45, ...), kind=kLoop, calls=%fused_computation.100 | loop fusion | flops 6815744 | bytes 13634688 | tf_op jit(solution)/shard_map/convert_element_type | solution.py:138
  120.0 0.9 copy.43
  (58 shorter events, 0.2 us)
Async XLA Ops:
  0.6 31.8 %copy-start = (bf16[32,32]{1,0:T(8,128)(2,1)S(1)}, bf16[32,32]{1,0:T(8,128)(2,1)}, u32[]{:S(2)}) copy-start(bf16[32,32]{1,0:T(8,128)(2,1)} %param.9) | copy-start | bytes 6148
  0.6 21.9 %copy-start.8 = (bf16[7,32,32]{2,1,0:T(8,128)(2,1)S(1)}, bf16[7,32,32]{2,1,0:T(8,128)(2,1)}, u32[]{:S(2)}) copy-start(bf16[7,32,32]{2,1,0:T(8,128)(2,1)} %param.10) | copy-start | bytes 43012
  3.8 17.8 %collective-permute-start.7 = (bf16[16,32,256]{2,1,0:T(8,128)(2,1)S(1)}, bf16[16,32,256]{2,1,0:T(8,128)(2,1)S(1)}, u32[]{:S(2)}, u32[]{:S(2)}) collective-permute-start(bf16[16,32,256]{2,1,0:T(8,128)(2,1)S(1)} %gather_fusion.2), channel_id=1, source_target_pairs={{8,0},{12,4},{0,8},{4,12},{9,1},{13,5},{1,9},{5,13},{10,2},{14,6},... | collective-permute-start | bytes 786440 | tf_op jit(solution)/shard_map/ppermute | solution.py:24
  7.9 19.0 %collective-permute-start.6 = (bf16[16,32,256]{2,1,0:T(8,128)(2,1)S(1)}, bf16[16,32,256]{2,1,0:T(8,128)(2,1)S(1)}, u32[]{:S(2)}, u32[]{:S(2)}) collective-permute-start(bf16[16,32,256]{2,1,0:T(8,128)(2,1)S(1)} %gather_fusion.2), channel_id=1, source_target_pairs={{4,0},{8,4},{12,8},{0,12},{5,1},{9,5},{13,9},{1,13},{6,2},{10,6},{... | collective-permute-start | bytes 786440 | tf_op jit(solution)/shard_map/ppermute | solution.py:24
  9.2 17.4 %collective-permute-start.5 = (bf16[16,32,256]{2,1,0:T(8,128)(2,1)S(1)}, bf16[16,32,256]{2,1,0:T(8,128)(2,1)S(1)}, u32[]{:S(2)}, u32[]{:S(2)}) collective-permute-start(bf16[16,32,256]{2,1,0:T(8,128)(2,1)S(1)} %gather_fusion.2), channel_id=1, source_target_pairs={{12,0},{0,4},{4,8},{8,12},{13,1},{1,5},{5,9},{9,13},{14,2},{2,6},{... | collective-permute-start | bytes 786440 | tf_op jit(solution)/shard_map/ppermute | solution.py:24
  10.9 17.6 %copy-start.3 = (bf16[16,32,2,128]{3,1,2,0:T(8,128)(2,1)}, bf16[16,32,2,128]{3,1,2,0:T(8,128)(2,1)S(1)}, u32[]{:S(2)}) copy-start(bf16[16,32,2,128]{3,1,2,0:T(8,128)(2,1)S(1)} %copy.27) | copy-start | bytes 786436
  10.9 17.6 %collective-permute-start.1 = (bf16[16,32,2,128]{3,1,2,0:T(8,128)(2,1)S(1)}, bf16[16,32,2,128]{3,1,2,0:T(8,128)(2,1)S(1)}, u32[]{:S(2)}, u32[]{:S(2)}) collective-permute-start(bf16[16,32,2,128]{3,1,2,0:T(8,128)(2,1)S(1)} %copy.27), channel_id=1, source_target_pairs={{1,0},{2,1},{3,2},{5,4},{6,5},{7,6},{9,8},{10,9},{11,10},{13,12},{... | collective-permute-start | bytes 786440 | tf_op jit(solution)/shard_map/ppermute | solution.py:16
  12.2 16.3 %collective-permute-start = (bf16[16,32,2,128]{3,1,2,0:T(8,128)(2,1)S(1)}, bf16[16,32,2,128]{3,1,2,0:T(8,128)(2,1)S(1)}, u32[]{:S(2)}, u32[]{:S(2)}) collective-permute-start(bf16[16,32,2,128]{3,1,2,0:T(8,128)(2,1)S(1)} %copy.27), channel_id=1, source_target_pairs={{0,1},{1,2},{2,3},{4,5},{5,6},{6,7},{8,9},{9,10},{10,11},{12,13},{... | collective-permute-start | bytes 786440 | tf_op jit(solution)/shard_map/ppermute | solution.py:13
  27.8 1.5 %copy-start.9 = (f32[32]{0:T(128)S(1)}, f32[32]{0:T(128)}, u32[]{:S(2)}) copy-start(f32[32]{0:T(128)} %get-tuple-element.55) | copy-start | bytes 388
  27.8 1.5 %copy-start.11 = (f32[32]{0:T(128)S(1)}, f32[32]{0:T(128)}, u32[]{:S(2)}) copy-start(f32[32]{0:T(128)} %get-tuple-element.56) | copy-start | bytes 388
  27.8 1.5 %copy-start.13 = (f32[32]{0:T(128)S(1)}, f32[32]{0:T(128)}, u32[]{:S(2)}) copy-start(f32[32]{0:T(128)} %get-tuple-element.57) | copy-start | bytes 388
  27.8 1.5 %copy-start.15 = (f32[32]{0:T(128)S(1)}, f32[32]{0:T(128)}, u32[]{:S(2)}) copy-start(f32[32]{0:T(128)} %get-tuple-element.58) | copy-start | bytes 388
  27.9 1.5 %copy-start.17 = (f32[32]{0:T(128)S(1)}, f32[32]{0:T(128)}, u32[]{:S(2)}) copy-start(f32[32]{0:T(128)} %get-tuple-element.59) | copy-start | bytes 388
  27.9 1.5 %copy-start.19 = (f32[32]{0:T(128)S(1)}, f32[32]{0:T(128)}, u32[]{:S(2)}) copy-start(f32[32]{0:T(128)} %get-tuple-element.60) | copy-start | bytes 388
  27.9 1.5 %copy-start.21 = (f32[32]{0:T(128)S(1)}, f32[32]{0:T(128)}, u32[]{:S(2)}) copy-start(f32[32]{0:T(128)} %get-tuple-element.61) | copy-start | bytes 388
  28.5 3.9 %copy-start.6 = (bf16[16,32,2,128]{3,1,2,0:T(8,128)(2,1)}, bf16[16,32,2,128]{3,1,2,0:T(8,128)(2,1)S(1)}, u32[]{:S(2)}) copy-start(bf16[16,32,2,128]{3,1,2,0:T(8,128)(2,1)S(1)} %collective-permute-done.1) | copy-start | bytes 786436
  28.5 0.8 copy-start.7
  32.4 11.1 %copy-start.4 = (bf16[16,32,2,128]{3,1,2,0:T(8,128)(2,1)S(1)}, bf16[16,32,2,128]{3,1,2,0:T(8,128)(2,1)}, u32[]{:S(2)}) copy-start(bf16[16,32,2,128]{3,1,2,0:T(8,128)(2,1)} %copy-done.3) | copy-start | bytes 786436
  34.2 27.5 %collective-permute-start.4 = (bf16[16,32,256]{2,1,0:T(8,128)(2,1)S(1)}, bf16[16,32,256]{2,1,0:T(8,128)(2,1)}, u32[]{:S(2)}, u32[]{:S(2)}) collective-permute-start(bf16[16,32,256]{2,1,0:T(8,128)(2,1)S(1)} %gather_fusion), channel_id=1, source_target_pairs={{8,0},{12,4},{0,8},{4,12},{9,1},{13,5},{1,9},{5,13},{10,2},{14,6},... | collective-permute-start | bytes 786440 | tf_op jit(solution)/shard_map/ppermute | solution.py:24
  41.3 19.0 %collective-permute-start.3 = (bf16[16,32,256]{2,1,0:T(8,128)(2,1)S(1)}, bf16[16,32,256]{2,1,0:T(8,128)(2,1)}, u32[]{:S(2)}, u32[]{:S(2)}) collective-permute-start(bf16[16,32,256]{2,1,0:T(8,128)(2,1)S(1)} %gather_fusion), channel_id=1, source_target_pairs={{4,0},{8,4},{12,8},{0,12},{5,1},{9,5},{13,9},{1,13},{6,2},{10,6},{... | collective-permute-start | bytes 786440 | tf_op jit(solution)/shard_map/ppermute | solution.py:24
  41.8 21.2 %collective-permute-start.2 = (bf16[16,32,256]{2,1,0:T(8,128)(2,1)S(1)}, bf16[16,32,256]{2,1,0:T(8,128)(2,1)}, u32[]{:S(2)}, u32[]{:S(2)}) collective-permute-start(bf16[16,32,256]{2,1,0:T(8,128)(2,1)S(1)} %gather_fusion), channel_id=1, source_target_pairs={{12,0},{0,4},{4,8},{8,12},{13,1},{1,5},{5,9},{9,13},{14,2},{2,6},{... | collective-permute-start | bytes 786440 | tf_op jit(solution)/shard_map/ppermute | solution.py:24
  46.0 6.8 %copy-start.5 = (bf16[16,32,2,128]{3,1,2,0:T(8,128)(2,1)S(1)}, bf16[16,32,2,128]{3,1,2,0:T(8,128)(2,1)}, u32[]{:S(2)}) copy-start(bf16[16,32,2,128]{3,1,2,0:T(8,128)(2,1)} %get-tuple-element.76) | copy-start | bytes 786436
  46.0 7.0 %copy-start.1 = (bf16[16,32,2,128]{3,2,1,0:T(2,128)(2,1)S(1)}, bf16[16,32,2,128]{3,2,1,0:T(2,128)(2,1)}, u32[]{:S(2)}) copy-start(bf16[16,32,2,128]{3,2,1,0:T(2,128)(2,1)} %param.6) | copy-start | bytes 786436
  48.4 67.7 %collective-permute-start.9 = (bf16[16,32,2,128]{3,1,2,0:T(8,128)(2,1)S(1)}, bf16[16,32,2,128]{3,1,2,0:T(8,128)(2,1)S(1)}, u32[]{:S(2)}, u32[]{:S(2)}) collective-permute-start(bf16[16,32,2,128]{3,1,2,0:T(8,128)(2,1)S(1)} %bitcast.337), channel_id=1, source_target_pairs={{1,0},{2,1},{3,2},{5,4},{6,5},{7,6},{9,8},{10,9},{11,10},{13,12},{... | collective-permute-start | bytes 786440 | tf_op jit(solution)/shard_map/ppermute | solution.py:16
  49.7 66.5 %collective-permute-start.8 = (bf16[16,32,2,128]{3,1,2,0:T(8,128)(2,1)S(1)}, bf16[16,32,2,128]{3,1,2,0:T(8,128)(2,1)S(1)}, u32[]{:S(2)}, u32[]{:S(2)}) collective-permute-start(bf16[16,32,2,128]{3,1,2,0:T(8,128)(2,1)S(1)} %bitcast.338), channel_id=1, source_target_pairs={{0,1},{1,2},{2,3},{4,5},{5,6},{6,7},{8,9},{9,10},{10,11},{12,13},{... | collective-permute-start | bytes 786440 | tf_op jit(solution)/shard_map/ppermute | solution.py:13
  113.6 3.3 %copy-start.2 = (bf16[16,32,2,128]{3,2,1,0:T(2,128)(2,1)S(1)}, bf16[16,32,2,128]{3,2,1,0:T(2,128)(2,1)}, u32[]{:S(2)}) copy-start(bf16[16,32,2,128]{3,2,1,0:T(2,128)(2,1)} %param.7) | copy-start | bytes 786436
  113.6 3.3 %copy-start.10 = (f32[32]{0:T(128)S(1)}, f32[32]{0:T(128)}, u32[]{:S(2)}) copy-start(f32[32]{0:T(128)} %get-tuple-element.55) | copy-start | bytes 388
  113.6 3.3 %copy-start.12 = (f32[32]{0:T(128)S(1)}, f32[32]{0:T(128)}, u32[]{:S(2)}) copy-start(f32[32]{0:T(128)} %get-tuple-element.56) | copy-start | bytes 388
  113.6 3.3 %copy-start.14 = (f32[32]{0:T(128)S(1)}, f32[32]{0:T(128)}, u32[]{:S(2)}) copy-start(f32[32]{0:T(128)} %get-tuple-element.57) | copy-start | bytes 388
  113.6 3.3 %copy-start.16 = (f32[32]{0:T(128)S(1)}, f32[32]{0:T(128)}, u32[]{:S(2)}) copy-start(f32[32]{0:T(128)} %get-tuple-element.58) | copy-start | bytes 388
  113.6 3.3 %copy-start.18 = (f32[32]{0:T(128)S(1)}, f32[32]{0:T(128)}, u32[]{:S(2)}) copy-start(f32[32]{0:T(128)} %get-tuple-element.59) | copy-start | bytes 388
  113.6 3.3 %copy-start.20 = (f32[32]{0:T(128)S(1)}, f32[32]{0:T(128)}, u32[]{:S(2)}) copy-start(f32[32]{0:T(128)} %get-tuple-element.60) | copy-start | bytes 388
  113.6 3.3 %copy-start.22 = (f32[32]{0:T(128)S(1)}, f32[32]{0:T(128)}, u32[]{:S(2)}) copy-start(f32[32]{0:T(128)} %get-tuple-element.61) | copy-start | bytes 388
